TPU v7x, 128 devices: a whole 4x4x4 slice. The times are simulated.
128 devices in a mesh: dp: 4 (over z_lo, core), tensor: 32 (over y, x, z_hi).
Axes of the slice: x: 4, y: 4, z: 4 (z_hi: 2, z_lo: 2; z = z_hi * 2 + z_lo), core: 2. Of those that a mesh axis runs over, the one named last changes fastest.
Arguments:
- stream: bfloat16 [6144, 2560], P(('dp', 'tensor')), may hold values from -26 to 26
- lengths: int32 [4, 6], P('dp'), may hold values from 16 to 768, as said below
- page_table: int32 [384], P('dp'), may hold values from 0 to 383, as said below
- request_prompt: int32 [64], P('dp'), may hold values from 0 to 23
- attn_gain: bfloat16 [2560], replicated, may hold values from 0.099609375 to 1.8984375
- query_gain: bfloat16 [128], replicated, may hold values from 0.5 to 10, as said below
- key_gain: bfloat16 [128], replicated, may hold values from 0.5 to 10, as said below
- mlp_gain: bfloat16 [2560], replicated, may hold values from 0.099609375 to 1.8984375
- w_query: bfloat16 [2560, 4096], P(None, 'tensor'), may hold values from -0.125 to 0.125
- key_value_weight: bfloat16 [2560, 2048], P(None, 'tensor'), may hold values from -0.125 to 0.125
- w_out: bfloat16 [4096, 2560], P('tensor'), may hold values from -0.5 to 0.5
- w_gate: bfloat16 [2560, 9728], P(None, 'tensor'), may hold values from -0.125 to 0.125
- w_up: bfloat16 [2560, 9728], P(None, 'tensor'), may hold values from -0.125 to 0.125
- w_down: bfloat16 [9728, 2560], P('tensor'), may hold values from -0.0625 to 0.0625
Outputs:
- layer_out: bfloat16 [6144, 2560], P(('dp', 'tensor'))
- paged_key_value_cache: bfloat16 [384, 16, 2048], P('dp', None, 'tensor')
- request_state: bfloat16 [64, 2560], P('dp', 'tensor')
Inputs may be any that keep to these rules, and one draw needn't show every extreme that they name: Every length is a multiple of 16; each batch's lengths add up to 1536, and the largest length of each batch is exactly 768. page_table is a permutation of all global slots; slot v belongs to owner v // 96, and each batch writes exactly 24 pages to each owner. `query_gain`: positive gains. `key_gain`: positive gains.
All inputs are finite; a program needn't handle non-finite values.
Results may differ from a plain program's by a relative error of at most 0.02.
The roundings to bfloat16 on the way count: a program that leaves them out, or rounds other values in their place, can miss the bound.
Values may be sent and summed in bfloat16 or wider, within the bound.
No kernel may reach another device: no remote copies, remote signals or barrier semaphores. Data moves between devices by JAX's collectives and lax.ppermute only.
A program may use at most 128 MiB of HBM per device.

v0:
```python
import math
import jax
import jax.numpy as jnp
from jax import lax
from jax.sharding import PartitionSpec as P

KEY_VALUE_HEADS = 8
HEAD_SIZE = 128
PAGE_TOKENS = 16
TENSOR = ("ty", "tx", "tz")
TENSOR_SHAPE = (4, 4, 2)
epsilon = 1e-06
rope_base = 1000000.0


def partner_2(value, axis, bit):
    mask = 2**bit
    pairs = [(source, source ^ mask) for source in range(lax.axis_size(axis))]
    return lax.ppermute(value, axis, pairs)


def scatter_sum(partial, parts):
    pieces = partial.reshape((parts, partial.shape[0] // parts) + partial.shape[1:])
    got = lax.all_to_all(pieces, TENSOR, 0, 0, tiled=True)
    return jnp.sum(got.astype(jnp.float32), axis=0)


def gather_rows(rows):
    rows = lax.all_gather(rows, "tz", axis=0, tiled=True)
    return lax.all_gather(rows, ("ty", "tx"), axis=0, tiled=True)


def row_norm(inputs, gain):
    inputs = inputs.astype(jnp.float32)
    scale = lax.rsqrt(jnp.mean(inputs * inputs, axis=-1, keepdims=True) + epsilon)
    return inputs * scale * gain.astype(jnp.float32)


def rotate(inputs, position):
    half_dim = inputs.shape[-1] // 2
    frequency = rope_base ** (-2.0 * jnp.arange(half_dim, dtype=jnp.float32) / inputs.shape[-1])
    angles = position.astype(jnp.float32)[:, None] * frequency[None, :]
    cosine = jnp.cos(angles)[:, None, :]
    sine_part = jnp.sin(angles)[:, None, :]
    front = inputs[..., :half_dim]
    second = inputs[..., half_dim:]
    return jnp.concatenate(
        [front * cosine - second * sine_part, second * cosine + front * sine_part], axis=-1
    )


def prompt_layout(lengths_row, token_count):
    prompt_ends = jnp.cumsum(lengths_row)
    prompt_starts = prompt_ends - lengths_row
    row_ids = jnp.arange(token_count, dtype=jnp.int32)
    prompt = jnp.sum((row_ids[:, None] >= prompt_ends[None, :]).astype(jnp.int32), axis=1)
    inside = (row_ids[:, None] >= prompt_starts[None, :]) & (
        row_ids[:, None] < prompt_ends[None, :]
    )
    offset = jnp.sum(jnp.where(inside, prompt_starts[None, :], 0), axis=1)
    return (prompt, row_ids - offset, prompt_starts, prompt_ends)


def per_device(
    stream,
    lengths,
    page_table,
    request_prompt,
    attn_gain,
    query_gain,
    key_gain,
    mlp_gain,
    w_query,
    key_value_weight,
    w_out,
    w_gate,
    w_up,
    w_down,
):
    tok_dev = stream.shape[0]
    tensor_element_count = lax.axis_size(TENSOR)
    token_count = tok_dev * tensor_element_count
    my_index = lax.axis_index(TENSOR)
    heads_dev = w_query.shape[1] // HEAD_SIZE
    query_cols = heads_dev * HEAD_SIZE
    prompt, position, prompt_starts, prompt_ends = prompt_layout(lengths[0], token_count)
    portion = gather_rows(row_norm(stream, attn_gain).astype(jnp.bfloat16))
    key_value_group = tensor_element_count // KEY_VALUE_HEADS
    head_weight = key_value_weight
    for bit_id in range(key_value_group.bit_length() - 1):
        partner = partner_2(head_weight, TENSOR, bit_id)
        upper_half = my_index // 2**bit_id % 2
        head_weight = jnp.where(
            upper_half == 1,
            jnp.concatenate([partner, head_weight], axis=1),
            jnp.concatenate([head_weight, partner], axis=1),
        )
    joined = jnp.concatenate(
        [
            jnp.dot(portion, w_query, preferred_element_type=jnp.float32),
            jnp.dot(portion, head_weight, preferred_element_type=jnp.float32),
        ],
        axis=1,
    )
    queries = joined[:, :query_cols].reshape(token_count, heads_dev, HEAD_SIZE)
    kv_part = joined[:, query_cols:].astype(jnp.bfloat16)
    key_flat = rotate(row_norm(kv_part[:, None, :HEAD_SIZE], key_gain), position).astype(
        jnp.bfloat16
    )[:, 0, :]
    value_matrix_rows = kv_part[:, HEAD_SIZE:]
    q_rot = rotate(row_norm(queries, query_gain), position).astype(jnp.bfloat16)
    piece_cols = key_value_weight.shape[1]
    head_rows = jnp.concatenate([key_flat, value_matrix_rows], axis=1)
    own_cols = lax.dynamic_slice_in_dim(
        head_rows, my_index % key_value_group * piece_cols, piece_cols, 1
    )
    page_count = token_count // PAGE_TOKENS
    page_rows = own_cols.reshape(page_count, PAGE_TOKENS, piece_cols)
    group_count = lax.axis_size("dp")
    capacity = page_count // group_count
    owners = page_table // page_count
    slot_ids = page_table % page_count
    hits = (owners[:, None] == jnp.arange(group_count, dtype=jnp.int32)[None, :]).astype(jnp.int32)
    order_in = jnp.sum((jnp.cumsum(hits, axis=0) - hits) * hits, axis=1)
    buffer_pos = owners * capacity + order_in
    source = (
        jnp.zeros((page_count,), jnp.int32)
        .at[buffer_pos]
        .set(jnp.arange(page_count, dtype=jnp.int32))
    )
    send_pages = page_rows[source].reshape(group_count, capacity, PAGE_TOKENS, piece_cols)
    send_slots = slot_ids[source].reshape(group_count, capacity)
    got_pages, got_slots = (
        lax.all_to_all(send_pages, "dp", split_axis=0, concat_axis=0, tiled=True),
        lax.all_to_all(send_slots, "dp", split_axis=0, concat_axis=0, tiled=True),
    )
    paged_key_value_cache = (
        jnp.zeros((page_count, PAGE_TOKENS, piece_cols), jnp.bfloat16)
        .at[got_slots.reshape(-1)]
        .set(got_pages.reshape(page_count, PAGE_TOKENS, piece_cols))
    )
    block_rows = min(512, token_count)
    block_total = token_count // block_rows
    score_scale = math.sqrt(HEAD_SIZE)
    all_ids = jnp.arange(token_count, dtype=jnp.int32)
    local_ids = jnp.arange(block_rows, dtype=jnp.int32)

    def dense_block(block_index):
        first_row = block_index * block_rows
        q_block = lax.dynamic_slice_in_dim(q_rot, first_row, block_rows, 0)
        q_prompt = lax.dynamic_slice_in_dim(prompt, first_row, block_rows, 0)
        row_ids = first_row + local_ids
        scores = (
            jnp.einsum("qhd,kd->hqk", q_block, key_flat, preferred_element_type=jnp.float32)
            / score_scale
        )
        allowed = ((q_prompt[:, None] == prompt[None, :]) & (row_ids[:, None] >= all_ids[None, :]))[
            None
        ]
        peak = jnp.max(jnp.where(allowed, scores, -jnp.inf), axis=2, keepdims=True)
        weight = jnp.where(allowed, jnp.exp(scores - peak), 0.0)
        total_weight = jnp.sum(weight, axis=2, keepdims=True)
        running = jnp.einsum(
            "hqk,kd->hqd",
            weight.astype(jnp.bfloat16),
            value_matrix_rows,
            preferred_element_type=jnp.float32,
        )
        return (running / total_weight).astype(jnp.bfloat16)

    block_ids = jnp.arange(block_total, dtype=jnp.int32)
    blocks_out = lax.map(dense_block, block_ids)
    attn = jnp.transpose(blocks_out, (0, 2, 1, 3)).reshape(token_count, query_cols)
    attn_sum = scatter_sum(
        jnp.dot(attn, w_out, preferred_element_type=jnp.float32).astype(jnp.bfloat16),
        tensor_element_count,
    )
    resid = (stream.astype(jnp.float32) + attn_sum).astype(jnp.bfloat16)
    portion = gather_rows(row_norm(resid, mlp_gain).astype(jnp.bfloat16))
    paged_key_value_cache, portion = lax.optimization_barrier((paged_key_value_cache, portion))
    gate_rows = jnp.dot(portion, w_gate, preferred_element_type=jnp.float32)
    upward = jnp.dot(portion, w_up, preferred_element_type=jnp.float32)
    hidden = (jax.nn.silu(gate_rows) * upward).astype(jnp.bfloat16)
    mlp_sum = scatter_sum(
        jnp.dot(hidden, w_down, preferred_element_type=jnp.float32).astype(jnp.bfloat16),
        tensor_element_count,
    )
    layer_out = (resid.astype(jnp.float32) + mlp_sum).astype(jnp.bfloat16)
    width = w_down.shape[1]
    feat = width // tensor_element_count
    nprompt = prompt_ends.shape[0]
    end_pick = ((prompt_ends - 1)[:, None] == all_ids[None, :]).astype(jnp.bfloat16)
    end_hidden = jnp.dot(end_pick, hidden, preferred_element_type=jnp.float32).astype(jnp.bfloat16)
    end_down = jnp.dot(end_hidden, w_down, preferred_element_type=jnp.float32).astype(jnp.bfloat16)
    my_rows = my_index * tok_dev + jnp.arange(tok_dev, dtype=jnp.int32)
    select = ((prompt_ends - 1)[:, None] == my_rows[None, :]).astype(jnp.bfloat16)
    end_resid = jnp.dot(select, resid, preferred_element_type=jnp.float32)
    end_terms = jnp.stack([end_down.astype(jnp.float32), end_resid])
    end_blocks = jnp.transpose(
        end_terms.reshape(2, nprompt, tensor_element_count, feat), (2, 0, 1, 3)
    )
    end_sums = lax.psum_scatter(end_blocks, TENSOR, scatter_dimension=0, tiled=True)[0]
    end_rows = (end_sums[0] + end_sums[1]).astype(jnp.bfloat16)
    table = lax.all_gather(end_rows, "dp", axis=0, tiled=True)
    pick = (request_prompt[:, None] == jnp.arange(table.shape[0], dtype=jnp.int32)[None, :]).astype(
        jnp.bfloat16
    )
    request_state = jnp.dot(pick, table, preferred_element_type=jnp.float32).astype(jnp.bfloat16)
    return (layer_out, paged_key_value_cache, request_state)


def solution(mesh):
    placed = (
        P(("dp",) + TENSOR, None),
        P("dp", None),
        P("dp"),
        P("dp"),
        P(),
        P(),
        P(),
        P(),
        P(None, TENSOR),
        P(None, TENSOR),
        P(TENSOR, None),
        P(None, TENSOR),
        P(None, TENSOR),
        P(TENSOR, None),
    )
    dp_size = mesh.shape["dp"]
    fine = jax.sharding.Mesh(mesh.devices.reshape((dp_size,) + TENSOR_SHAPE), ("dp",) + TENSOR)
    return jax.shard_map(
        per_device,
        mesh=fine,
        in_specs=placed,
        out_specs=(P(("dp",) + TENSOR, None), P("dp", None, TENSOR), P("dp", TENSOR)),
        check_vma=False,
    )
```

profile of v0, /device:TPU:1, one launch (start us, length us, event | category | flops | bytes accessed | tf_op | source)
XLA Modules:
  0.0 795.8 jit_solution(10298598283091658743)
XLA Ops:
  10.2 10.8 %all_gather.15 = bf16[96,2560]{1,0:T(8,128)(2,1)} all-gather(bf16[48,2560]{1,0:T(8,128)(2,1)S(1)} %fusion.48), channel_id=1, replica_groups=mesh['dp'=4,'ty'=4,'tx'=4,'tz'=2] {'tz'}, dimensions={0}, use_global_device_ids=true | all-gather | bytes 737280 | tf_op jit(solution)/shard_map/all_gather | solution.py:29
  27.1 3.8 collective-permute-done
  34.1 20.9 %collective-permute-done.1 = bf16[2560,128]{0,1:T(8,128)(2,1)} collective-permute-done((bf16[2560,128]{0,1:T(8,128)(2,1)S(1)}, bf16[2560,128]{0,1:T(8,128)(2,1)}, u32[]{:S(2)}, u32[]{:S(2)}) %collective-permute-start.1) | collective-permute-done | bytes 655392 | tf_op jit(solution)/shard_map/ppermute | solution.py:19
  54.9 41.6 %all-gather.4.cloned.1.call-done = bf16[1536,2560]{1,0:T(8,128)(2,1)} async-done(((bf16[96,2560]{1,0:T(8,128)(2,1)}), bf16[1536,2560]{1,0:T(8,128)(2,1)}) %all-gather.4.cloned.1.call-update) | async-done | bytes 7864336 | tf_op jit(solution)/shard_map/all_gather | solution.py:30
  96.5 5.9 convolution_convert_fusion.3
  102.6 3.8 multiply_reduce_fusion
  113.1 18.2 %while.11 = (s32[]{:T(128)}, bf16[3,1,512,128]{3,2,1,0:T(8,128)(2,1)S(1)}, s32[3]{0:T(128)S(1)}, s32[1536]{0:T(1024)S(1)}, bf16[1536,1,128]{0,2,1:T(8,128)(2,1)}...) while((s32[]{:T(128)}, ...), condition=%wide.region_9.10_spmd.clone, body=%wide.region_6.9_spmd.clone.sunk | while | flops 416939520 | bytes 12107995 | solution.py:172
  131.4 5.3 convolution_convert_fusion.1
  136.7 8.1 %all-to-all-start = ((bf16[32,48,2560]{2,1,0:T(8,128)(2,1)}), bf16[32,48,2560]{2,1,0:T(8,128)(2,1)}, u32[]{:S(2)}, u32[]{:S(2)}) async-start(bf16[32,48,2560]{2,1,0:T(8,128)(2,1)} %bitcast.96), calls=%async_computation | async-start | bytes 15728640 | tf_op jit(solution)/shard_map/all_to_all | solution.py:24
  145.1 115.4 %all-to-all-done = bf16[32,48,2560]{2,1,0:T(8,128)(2,1)} async-done(((bf16[32,48,2560]{2,1,0:T(8,128)(2,1)}), bf16[32,48,2560]{2,1,0:T(8,128)(2,1)}, u32[]{:S(2)}, u32[]{:S(2)}) %all-to-all-start) | async-done | bytes 7864352 | tf_op jit(solution)/shard_map/all_to_all | solution.py:24
  260.4 4.5 convert_reduce_fusion.1
  265.3 7.8 all_gather.17
  276.4 6.0 all-to-all-start.1
  282.4 3.0 all-to-all-done.1
  288.8 4.0 all-to-all-start.2
  292.8 4.5 all-to-all-done.2
  297.6 3.5 scatter_fusion
  301.1 47.3 %all-gather.6.cloned.1.call-done = bf16[1536,2560]{1,0:T(8,128)(2,1)} async-done(((bf16[96,2560]{1,0:T(8,128)(2,1)}), bf16[1536,2560]{1,0:T(8,128)(2,1)}) %all-gather.6.cloned.1.call-update) | async-done | bytes 7864336 | tf_op jit(solution)/shard_map/all_gather | solution.py:30
  348.4 5.6 fusion.84
  357.4 6.5 convolution_convert_fusion
  363.9 8.1 %all-to-all-start.3 = ((bf16[32,48,2560]{2,1,0:T(8,128)(2,1)}), bf16[32,48,2560]{2,1,0:T(8,128)(2,1)}, u32[]{:S(2)}, u32[]{:S(2)}) async-start(bf16[32,48,2560]{2,1,0:T(8,128)(2,1)} %bitcast.97), calls=%async_computation.3 | async-start | bytes 15728640 | tf_op jit(solution)/shard_map/all_to_all | solution.py:24
  376.1 380.2 %all-reduce.3.cloned.1.call-done = f32[32,2,6,80]{3,1,0,2:T(2,128)} async-done(((f32[32,2,6,80]{3,1,0,2:T(2,128)}), f32[32,2,6,80]{3,1,0,2:T(2,128)}) %all-reduce.3.cloned.1.call-update) | async-done | bytes 122896
  757.8 25.4 %all-gather = bf16[1,1,24,80]{3,1,0,2:T(2,128)(2,1)S(1)} all-gather(bf16[1,1,6,80]{3,1,0,2:T(2,128)(2,1)S(1)} %fusion.75), channel_id=2, replica_groups=mesh['dp'=4,'ty'=4,'tx'=4,'tz'=2] {'dp'}, dimensions={2}, use_global_device_ids=true | all-gather | bytes 4800 | tf_op jit(solution)/shard_map/all_gather | solution.py:204
  783.9 4.5 convert_reduce_fusion
  (124 shorter events, 53.0 us)
Async XLA Ops:
  7.2 350.2 %copy-start = (bf16[304,2560]{1,0:T(8,128)(2,1)S(1)}, bf16[304,2560]{1,0:T(8,128)(2,1)}, u32[]{:S(2)}) copy-start(bf16[304,2560]{1,0:T(8,128)(2,1)} %param.29) | copy-start | bytes 4669444
  7.2 26.8 %copy-start.11 = (s32[1,6]{1,0:T(1,128)S(1)}, s32[1,6]{1,0:T(1,128)}, u32[]{:S(2)}) copy-start(s32[1,6]{1,0:T(1,128)} %param.17) | copy-start | bytes 76
  7.2 89.3 %all-gather.4.cloned.1.call-start = ((), (), s32[]{:S(2)}) async-start(), calls=%async_computation.4 | async-start | bytes 8355840 | tf_op jit(solution)/shard_map/all_gather | solution.py:30
  21.1 9.8 %collective-permute-start = (bf16[2560,64]{0,1:T(8,128)(2,1)}, bf16[2560,64]{0,1:T(8,128)(2,1)S(1)}, u32[]{:S(2)}, u32[]{:S(2)}) collective-permute-start(bf16[2560,64]{0,1:T(8,128)(2,1)} %param.25), channel_id=1, source_target_pairs={{0,1},{1,0},{2,3},{3,2},{4,5},{5,4},{6,7},{7,6},{8,9},{9,8},{10,11... | collective-permute-start | bytes 983048 | tf_op jit(solution)/shard_map/ppermute | solution.py:19
  24.7 77.7 %copy-start.7 = (s32[6,1]{0,1:T(1,128)}, s32[6,1]{0,1:T(1,128)S(1)}, u32[]{:S(2)}) copy-start(s32[6,1]{0,1:T(1,128)S(1)} %reduce-window.4) | copy-start | bytes 76
  32.1 22.8 %collective-permute-start.1 = (bf16[2560,128]{0,1:T(8,128)(2,1)S(1)}, bf16[2560,128]{0,1:T(8,128)(2,1)}, u32[]{:S(2)}, u32[]{:S(2)}) collective-permute-start(bf16[2560,128]{0,1:T(8,128)(2,1)S(1)} %maximum_select_fusion.2), channel_id=1, source_target_pairs={{0,2},{1,3},{2,0},{3,1},{4,6},{5,7},{6,4},{7,5},{8,10},{9,11},{10,... | collective-permute-start | bytes 1966088 | tf_op jit(solution)/shard_map/ppermute | solution.py:19
  96.5 6.0 copy-start.1
  108.1 5.0 copy-start.3
  113.1 18.2 %copy-start.4 = (bf16[128,2560]{1,0:T(8,128)(2,1)S(1)}, bf16[128,2560]{1,0:T(8,128)(2,1)}, u32[]{:S(2)}) copy-start(bf16[128,2560]{1,0:T(8,128)(2,1)} %param.26) | copy-start | bytes 1966084
  120.5 3.2 copy-start.5
  126.6 3.2 copy-start.5
  136.7 8.3 %copy-start.6 = (bf16[2560]{0:T(1024)(128)(2,1)S(1)}, bf16[2560]{0:T(1024)(128)(2,1)}, u32[]{:S(2)}) copy-start(bf16[2560]{0:T(1024)(128)(2,1)} %param.23) | copy-start | bytes 15364
  136.7 123.7 %all-to-all-start = ((bf16[32,48,2560]{2,1,0:T(8,128)(2,1)}), bf16[32,48,2560]{2,1,0:T(8,128)(2,1)}, u32[]{:S(2)}, u32[]{:S(2)}) async-start(bf16[32,48,2560]{2,1,0:T(8,128)(2,1)} %bitcast.96), calls=%async_computation | async-start | bytes 15728640 | tf_op jit(solution)/shard_map/all_to_all | solution.py:24
  144.8 203.5 %all-gather.6.cloned.1.call-start = ((), (), s32[]{:S(2)}) async-start(), calls=%async_computation.5 | async-start | bytes 8355840 | tf_op jit(solution)/shard_map/all_gather | solution.py:30
  145.1 119.9 %copy-start.2 = (bf16[48,2560]{1,0:T(8,128)(2,1)S(1)}, bf16[48,2560]{1,0:T(8,128)(2,1)}, u32[]{:S(2)}) copy-start(bf16[48,2560]{1,0:T(8,128)(2,1)} %param.16) | copy-start | bytes 737284
  145.1 128.1 %copy-start.12 = (s32[96]{0:T(128)S(1)}, s32[96]{0:T(128)}, u32[]{:S(2)}) copy-start(s32[96]{0:T(128)} %param.18) | copy-start | bytes 1156
  276.4 9.0 %all-to-all-start.1 = ((s32[4,1,24]{2,1,0:T(1,128)}), s32[4,1,24]{2,1,0:T(1,128)S(1)}, u32[]{:S(2)}, u32[]{:S(2)}) async-start(s32[4,1,24]{2,1,0:T(1,128)} %bitcast.10), calls=%async_computation.1 | async-start | bytes 4096 | tf_op jit(solution)/shard_map/all_to_all | solution.py:135
  288.8 8.5 %all-to-all-start.2 = ((bf16[4,2,12288]{2,1,0:T(2,128)(2,1)}), bf16[4,2,12288]{2,1,0:T(2,128)(2,1)S(1)}, u32[]{:S(2)}, u32[]{:S(2)}) async-start(bf16[4,2,12288]{2,1,0:T(2,128)(2,1)} %reshape.459), calls=%async_computation.2 | async-start | bytes 393216 | tf_op jit(solution)/shard_map/all_to_all | solution.py:134
  348.3 6.0 copy-start.9
  348.4 6.4 copy-start.10
  363.9 8.2 %copy-start.8 = (s32[6,1]{0,1:T(1,128)S(1)}, s32[6,1]{0,1:T(1,128)}, u32[]{:S(2)}) copy-start(s32[6,1]{0,1:T(1,128)} %copy-done.7) | copy-start | bytes 76
  363.9 420.0 %all-to-all-start.3 = ((bf16[32,48,2560]{2,1,0:T(8,128)(2,1)}), bf16[32,48,2560]{2,1,0:T(8,128)(2,1)}, u32[]{:S(2)}, u32[]{:S(2)}) async-start(bf16[32,48,2560]{2,1,0:T(8,128)(2,1)} %bitcast.97), calls=%async_computation.3 | async-start | bytes 15728640 | tf_op jit(solution)/shard_map/all_to_all | solution.py:24
  372.0 411.1 %copy-start.13 = (s32[16]{0:T(128)S(1)}, s32[16]{0:T(128)}, u32[]{:S(2)}) copy-start(s32[16]{0:T(128)} %param.19) | copy-start | bytes 196
  372.0 384.3 %all-reduce.3.cloned.1.call-start = ((), (), s32[]{:S(2)}) async-start(), calls=%async_computation.6 | async-start | bytes 393216
  (2 other events, 5.7 us)
Sparse Core Ops, SparseCore 0:
  21.2 75.2 all-gather.3
  273.3 74.9 all-gather.5
  375.9 380.3 all-reduce.2
where the time goes:
time: 797 us; the launch traced here: 796 us
  waiting for transfers between devices  617 us (77%)
  blocking collectives  44.1 us (6%)
  matrix products  42.8 us (5%)
  starting transfers between devices  30.6 us (4%)
  other arithmetic  29.9 us (4%)
  local copies, waits for them, and re-layouts  15.6 us (2%)
  between operations  14.2 us (2%)
    unnamed x4, waiting for transfers between devices  380 us
    all_to_all x2, waiting for transfers between devices, scatter_sum(): got = lax.all_to_all(pieces, TENSOR, 0, 0, tiled=True)  115 us
    all_gather x2, waiting for transfers between devices, gather_rows(): return lax.all_gather(rows, ('ty', 'tx'), axis=0, tiled=True)  88.8 us
    all_gather x1, blocking collectives, per_device(): table = lax.all_gather(end_rows, 'dp', axis=0, tiled=True)  25.4 us
    ppermute x2, waiting for transfers between devices, partner_2(): return lax.ppermute(value, axis, pairs)  24.7 us
    all_gather x2, blocking collectives, gather_rows(): rows = lax.all_gather(rows, 'tz', axis=0, tiled=True)  18.7 us
    all_to_all x2, starting transfers between devices, scatter_sum(): got = lax.all_to_all(pieces, TENSOR, 0, 0, tiled=True)  16.2 us
  transfers between devices with their start and end apart: 9, of which 8 were waited for; matrix products, arithmetic and copies ran while one was open for 3% of the time, Pallas kernels for 0%

commit v1 on v0

--- a/solution.py
+++ b/solution.py
@@ -1,3 +1,4 @@
+import functools
 import math
 import jax
 import jax.numpy as jnp
@@ -11,6 +12,20 @@
 TENSOR_SHAPE = (4, 4, 2)
 epsilon = 1e-06
 rope_base = 1000000.0
+
+
+def _create_squares(in_array, mesh_name, out_dim):
+    before = lax.all_to_all(
+        jnp.stack([in_array for _ in range(lax.axis_size(mesh_name))], axis=0),
+        concat_axis=0,
+        split_axis=0,
+        axis_name=mesh_name,
+    )
+    b_next = jnp.concatenate(before, axis=out_dim)
+    return b_next
+
+
+match_the_shelves = functools.partial(_create_squares, mesh_name="dp", out_dim=0)
 
 
 def partner_2(value, axis, bit):
@@ -201,7 +216,7 @@
     )
     end_sums = lax.psum_scatter(end_blocks, TENSOR, scatter_dimension=0, tiled=True)[0]
     end_rows = (end_sums[0] + end_sums[1]).astype(jnp.bfloat16)
-    table = lax.all_gather(end_rows, "dp", axis=0, tiled=True)
+    table = match_the_shelves(end_rows)
     pick = (request_prompt[:, None] == jnp.arange(table.shape[0], dtype=jnp.int32)[None, :]).astype(
         jnp.bfloat16
     )

time: 797 us -> 701 us (0.88)
  waiting for transfers between devices: 617 us -> 514 us
  starting transfers between devices: 30.6 us -> 57 us
  blocking collectives: 44.1 us -> 18.7 us
    unnamed x4 -> x3, waiting for transfers between devices: 380 us -> 0.05 us
    reduce_scatter x0 -> x1, waiting for transfers between devices: none -> 160 us  [per_device(): lax.psum_scatter(end_blocks, TENSOR, scatter_dimension=0, tiled=True)[0]]
    all_to_all x2, waiting for transfers between devices: 115 us -> 233 us  [scatter_sum(): got = lax.all_to_all(pieces, TENSOR, 0, 0, tiled=True)]
    all_to_all x0 -> x1, starting transfers between devices: none -> 29.6 us  [_create_squares(): lax.all_to_all(jnp.stack([in_array for _ in range(lax.axis_size(mesh_name...]
    all_gather x1 -> x0, blocking collectives: 25.4 us -> none  [per_device(): table = lax.all_gather(end_rows, 'dp', axis=0, tiled=True)]
  transfers between devices with their start and end apart: 9 -> 10, of which waited for: 8 -> 9; matrix products, arithmetic and copies ran while one was open for 3% -> 3% of each run, Pallas kernels for 0% -> 0%
where the time goes in v1:
time: 701 us; the launch traced here: 693 us
  waiting for transfers between devices  514 us (73%)
  starting transfers between devices  57 us (8%)
  matrix products  42.7 us (6%)
  other arithmetic  29 us (4%)
  blocking collectives  18.7 us (3%)
  local copies, waits for them, and re-layouts  15.9 us (2%)
  between operations  14.2 us (2%)
    all_to_all x2, waiting for transfers between devices, scatter_sum(): got = lax.all_to_all(pieces, TENSOR, 0, 0, tiled=True)  233 us
    reduce_scatter x1, waiting for transfers between devices, per_device(): lax.psum_scatter(end_blocks, TENSOR, scatter_dimension=0, tiled=True)[0]  160 us
    all_gather x2, waiting for transfers between devices, gather_rows(): return lax.all_gather(rows, ('ty', 'tx'), axis=0, tiled=True)  88.5 us
    all_to_all x1, starting transfers between devices, _create_squares(): lax.all_to_all(jnp.stack([in_array for _ in range(lax.axis_size(mesh_name...  29.6 us
    ppermute x2, waiting for transfers between devices, partner_2(): return lax.ppermute(value, axis, pairs)  24.7 us
    all_gather x2, blocking collectives, gather_rows(): rows = lax.all_gather(rows, 'tz', axis=0, tiled=True)  18.7 us
  transfers between devices with their start and end apart: 10, of which 9 were waited for; matrix products, arithmetic and copies ran while one was open for 3% of the time, Pallas kernels for 0%

profile of v1, /device:TPU:1, one launch (start us, length us, event | category | flops | bytes accessed | tf_op | source)
XLA Modules:
  0.0 693.3 jit_solution(16706069264874183073)
XLA Ops:
  10.2 10.8 %all_gather.12 = bf16[96,2560]{1,0:T(8,128)(2,1)} all-gather(bf16[48,2560]{1,0:T(8,128)(2,1)S(1)} %fusion.48), channel_id=1, replica_groups=mesh['dp'=4,'ty'=4,'tx'=4,'tz'=2] {'tz'}, dimensions={0}, use_global_device_ids=true | all-gather | bytes 737280 | tf_op jit(solution)/shard_map/all_gather | solution.py:44
  27.1 3.8 collective-permute-done
  34.1 20.9 %collective-permute-done.1 = bf16[2560,128]{0,1:T(8,128)(2,1)} collective-permute-done((bf16[2560,128]{0,1:T(8,128)(2,1)S(1)}, bf16[2560,128]{0,1:T(8,128)(2,1)}, u32[]{:S(2)}, u32[]{:S(2)}) %collective-permute-start.1) | collective-permute-done | bytes 655392 | tf_op jit(solution)/shard_map/ppermute | solution.py:34
  54.9 41.6 %all-gather.3.cloned.1.call-done = bf16[1536,2560]{1,0:T(8,128)(2,1)} async-done(((bf16[96,2560]{1,0:T(8,128)(2,1)}), bf16[1536,2560]{1,0:T(8,128)(2,1)}) %all-gather.3.cloned.1.call-update) | async-done | bytes 7864336 | tf_op jit(solution)/shard_map/all_gather | solution.py:45
  96.5 5.9 convolution_convert_fusion.3
  102.6 3.8 multiply_reduce_fusion
  113.1 18.2 %while.11 = (s32[]{:T(128)}, bf16[3,1,512,128]{3,2,1,0:T(8,128)(2,1)S(1)}, s32[3]{0:T(128)S(1)}, s32[1536]{0:T(1024)S(1)}, bf16[1536,1,128]{0,2,1:T(8,128)(2,1)}...) while((s32[]{:T(128)}, ...), condition=%wide.region_9.10_spmd.clone, body=%wide.region_6.9_spmd.clone.sunk | while | flops 416939520 | bytes 12107995 | solution.py:187
  131.4 5.3 convolution_convert_fusion.1
  136.7 8.1 %all-to-all-start = ((bf16[32,48,2560]{2,1,0:T(8,128)(2,1)}), bf16[32,48,2560]{2,1,0:T(8,128)(2,1)}, u32[]{:S(2)}, u32[]{:S(2)}) async-start(bf16[32,48,2560]{2,1,0:T(8,128)(2,1)} %bitcast.89), calls=%async_computation | async-start | bytes 15728640 | tf_op jit(solution)/shard_map/all_to_all | solution.py:39
  145.1 115.3 %all-to-all-done = bf16[32,48,2560]{2,1,0:T(8,128)(2,1)} async-done(((bf16[32,48,2560]{2,1,0:T(8,128)(2,1)}), bf16[32,48,2560]{2,1,0:T(8,128)(2,1)}, u32[]{:S(2)}, u32[]{:S(2)}) %all-to-all-start) | async-done | bytes 7864352 | tf_op jit(solution)/shard_map/all_to_all | solution.py:39
  260.4 4.5 convert_reduce_fusion.1
  265.3 7.9 %all_gather.14 = bf16[96,2560]{1,0:T(8,128)(2,1)} all-gather(bf16[48,2560]{1,0:T(8,128)(2,1)S(1)} %fusion.52), channel_id=1, replica_groups=mesh['dp'=4,'ty'=4,'tx'=4,'tz'=2] {'tz'}, dimensions={0}, use_global_device_ids=true | all-gather | bytes 737280 | tf_op jit(solution)/shard_map/all_gather | solution.py:44
  276.4 6.0 all-to-all-start.1
  288.7 4.0 all-to-all-start.2
  292.8 4.5 all-to-all-done.2
  297.6 3.5 scatter_fusion
  301.5 46.9 %all-gather.5.cloned.1.call-done = bf16[1536,2560]{1,0:T(8,128)(2,1)} async-done(((bf16[96,2560]{1,0:T(8,128)(2,1)}), bf16[1536,2560]{1,0:T(8,128)(2,1)}) %all-gather.5.cloned.1.call-update) | async-done | bytes 7864336 | tf_op jit(solution)/shard_map/all_gather | solution.py:45
  348.4 5.6 fusion.83
  359.4 159.9 %reduce-scatter.2.cloned.1.call-done = f32[1,2,6,80]{3,2,1,0:T(8,128)} async-done(((f32[32,2,6,80]{3,2,1,0:T(8,128)}), f32[1,2,6,80]{3,2,1,0:T(8,128)}) %reduce-scatter.2.cloned.1.call-update) | async-done | bytes 3856 | tf_op jit(solution)/shard_map/reduce_scatter | solution.py:217
  520.6 29.6 %all-to-all-start.4 = ((bf16[4,2,240]{2,1,0:T(2,128)(2,1)}), bf16[4,2,240]{2,1,0:T(2,128)(2,1)S(1)}, u32[]{:S(2)}, u32[]{:S(2)}) async-start(bf16[4,2,240]{2,1,0:T(2,128)(2,1)} %reshape.466), calls=%async_computation.5 | async-start | bytes 8192 | tf_op jit(solution)/shard_map/all_to_all | solution.py:18
  550.2 6.5 convolution_convert_fusion
  556.6 5.1 all-to-all-start.3
  563.7 117.9 %all-to-all-done.3 = bf16[32,48,2560]{2,1,0:T(8,128)(2,1)} async-done(((bf16[32,48,2560]{2,1,0:T(8,128)(2,1)}), bf16[32,48,2560]{2,1,0:T(8,128)(2,1)}, u32[]{:S(2)}, u32[]{:S(2)}) %all-to-all-start.3) | async-done | bytes 7864352 | tf_op jit(solution)/shard_map/all_to_all | solution.py:39
  681.5 4.5 convert_reduce_fusion
  (128 shorter events, 55.3 us)
Async XLA Ops:
  7.2 350.3 %copy-start = (bf16[304,2560]{1,0:T(8,128)(2,1)S(1)}, bf16[304,2560]{1,0:T(8,128)(2,1)}, u32[]{:S(2)}) copy-start(bf16[304,2560]{1,0:T(8,128)(2,1)} %param.29) | copy-start | bytes 4669444
  7.2 26.7 %copy-start.11 = (s32[1,6]{1,0:T(1,128)S(1)}, s32[1,6]{1,0:T(1,128)}, u32[]{:S(2)}) copy-start(s32[1,6]{1,0:T(1,128)} %param.17) | copy-start | bytes 76
  7.2 89.3 %all-gather.3.cloned.1.call-start = ((), (), s32[]{:S(2)}) async-start(), calls=%async_computation.6 | async-start | bytes 8355840 | tf_op jit(solution)/shard_map/all_gather | solution.py:45
  21.1 9.8 %collective-permute-start = (bf16[2560,64]{0,1:T(8,128)(2,1)}, bf16[2560,64]{0,1:T(8,128)(2,1)S(1)}, u32[]{:S(2)}, u32[]{:S(2)}) collective-permute-start(bf16[2560,64]{0,1:T(8,128)(2,1)} %param.25), channel_id=1, source_target_pairs={{0,1},{1,0},{2,3},{3,2},{4,5},{5,4},{6,7},{7,6},{8,9},{9,8},{10,11... | collective-permute-start | bytes 983048 | tf_op jit(solution)/shard_map/ppermute | solution.py:34
  24.7 77.7 %copy-start.7 = (s32[6,1]{0,1:T(1,128)}, s32[6,1]{0,1:T(1,128)S(1)}, u32[]{:S(2)}) copy-start(s32[6,1]{0,1:T(1,128)S(1)} %reduce-window.4) | copy-start | bytes 76
  32.1 22.8 %collective-permute-start.1 = (bf16[2560,128]{0,1:T(8,128)(2,1)S(1)}, bf16[2560,128]{0,1:T(8,128)(2,1)}, u32[]{:S(2)}, u32[]{:S(2)}) collective-permute-start(bf16[2560,128]{0,1:T(8,128)(2,1)S(1)} %maximum_select_fusion.2), channel_id=1, source_target_pairs={{0,2},{1,3},{2,0},{3,1},{4,6},{5,7},{6,4},{7,5},{8,10},{9,11},{10,... | collective-permute-start | bytes 1966088 | tf_op jit(solution)/shard_map/ppermute | solution.py:34
  96.5 6.0 copy-start.1
  108.1 5.0 copy-start.3
  113.1 18.2 %copy-start.4 = (bf16[128,2560]{1,0:T(8,128)(2,1)S(1)}, bf16[128,2560]{1,0:T(8,128)(2,1)}, u32[]{:S(2)}) copy-start(bf16[128,2560]{1,0:T(8,128)(2,1)} %param.26) | copy-start | bytes 1966084
  126.6 3.2 copy-start.5
  136.7 8.3 %copy-start.6 = (bf16[2560]{0:T(1024)(128)(2,1)S(1)}, bf16[2560]{0:T(1024)(128)(2,1)}, u32[]{:S(2)}) copy-start(bf16[2560]{0:T(1024)(128)(2,1)} %param.23) | copy-start | bytes 15364
  136.7 123.7 %all-to-all-start = ((bf16[32,48,2560]{2,1,0:T(8,128)(2,1)}), bf16[32,48,2560]{2,1,0:T(8,128)(2,1)}, u32[]{:S(2)}, u32[]{:S(2)}) async-start(bf16[32,48,2560]{2,1,0:T(8,128)(2,1)} %bitcast.89), calls=%async_computation | async-start | bytes 15728640 | tf_op jit(solution)/shard_map/all_to_all | solution.py:39
  144.8 203.6 %all-gather.5.cloned.1.call-start = ((), (), s32[]{:S(2)}) async-start(), calls=%async_computation.7 | async-start | bytes 8355840 | tf_op jit(solution)/shard_map/all_gather | solution.py:45
  145.1 119.9 %copy-start.2 = (bf16[48,2560]{1,0:T(8,128)(2,1)S(1)}, bf16[48,2560]{1,0:T(8,128)(2,1)}, u32[]{:S(2)}) copy-start(bf16[48,2560]{1,0:T(8,128)(2,1)} %param.16) | copy-start | bytes 737284
  145.1 128.1 %copy-start.12 = (s32[96]{0:T(128)S(1)}, s32[96]{0:T(128)}, u32[]{:S(2)}) copy-start(s32[96]{0:T(128)} %param.18) | copy-start | bytes 1156
  265.0 17.5 %copy-start.8 = (s32[6,1]{0,1:T(1,128)S(1)}, s32[6,1]{0,1:T(1,128)}, u32[]{:S(2)}) copy-start(s32[6,1]{0,1:T(1,128)} %copy-done.7) | copy-start | bytes 76
  276.4 9.0 %all-to-all-start.1 = ((s32[4,1,24]{2,1,0:T(1,128)}), s32[4,1,24]{2,1,0:T(1,128)S(1)}, u32[]{:S(2)}, u32[]{:S(2)}) async-start(s32[4,1,24]{2,1,0:T(1,128)} %bitcast.10), calls=%async_computation.1 | async-start | bytes 4096 | tf_op jit(solution)/shard_map/all_to_all | solution.py:150
  288.7 8.5 %all-to-all-start.2 = ((bf16[4,2,12288]{2,1,0:T(2,128)(2,1)}), bf16[4,2,12288]{2,1,0:T(2,128)(2,1)S(1)}, u32[]{:S(2)}, u32[]{:S(2)}) async-start(bf16[4,2,12288]{2,1,0:T(2,128)(2,1)} %reshape.464), calls=%async_computation.2 | async-start | bytes 393216 | tf_op jit(solution)/shard_map/all_to_all | solution.py:149
  292.8 226.4 %reduce-scatter.2.cloned.1.call-start = ((), (), s32[]{:S(2)}) async-start(), calls=%async_computation.8 | async-start | bytes 270336 | tf_op jit(solution)/shard_map/reduce_scatter | solution.py:217
  348.4 6.0 copy-start.9
  348.4 6.4 copy-start.10
  520.6 36.0 %all-to-all-start.4 = ((bf16[4,2,240]{2,1,0:T(2,128)(2,1)}), bf16[4,2,240]{2,1,0:T(2,128)(2,1)S(1)}, u32[]{:S(2)}, u32[]{:S(2)}) async-start(bf16[4,2,240]{2,1,0:T(2,128)(2,1)} %reshape.466), calls=%async_computation.5 | async-start | bytes 8192 | tf_op jit(solution)/shard_map/all_to_all | solution.py:18
  556.6 6.2 copy-start.13
  556.6 124.9 %all-to-all-start.3 = ((bf16[32,48,2560]{2,1,0:T(8,128)(2,1)}), bf16[32,48,2560]{2,1,0:T(8,128)(2,1)}, u32[]{:S(2)}, u32[]{:S(2)}) async-start(bf16[32,48,2560]{2,1,0:T(8,128)(2,1)} %bitcast.90), calls=%async_computation.3 | async-start | bytes 15728640 | tf_op jit(solution)/shard_map/all_to_all | solution.py:39
  (2 other events, 6.5 us)
Sparse Core Ops, SparseCore 0:
  21.2 75.2 all-gather.2
  273.3 75.0 all-gather.4
  359.5 159.6 reduce-scatter.1
